TPU v7x, 32 devices: a whole 2x2x4 slice. The times are simulated.
32 devices in a mesh: req: 8 (over y, x, core), kv: 4 (over z).
Axes of the slice: x: 2, y: 2, z: 4, core: 2. Of those that a mesh axis runs over, the one named last changes fastest.
Arguments:
- hidden: bfloat16 [128, 8192], P('req', 'kv')
- cache_len: int32 [2, 128], replicated, may hold values from 1 to 4096, as said below
- request_serving_order: int32 [128], replicated, may hold values from 0 to 127, as said below
- rotated_key_cache: bfloat16 [2, 65536, 1024], P(None, 'req', 'kv'), as said below
- stored_value_cache: bfloat16 [2, 65536, 1024], P(None, 'req', 'kv'), may hold values from -6 to 6
- attn_gain: bfloat16 [8192], P('kv'), may hold values from 0.099609375 to 1.8984375
- w_query: bfloat16 [8192, 8192], P('req', 'kv'), may hold values from -0.0625 to 0.0625
- key_projection_weight: bfloat16 [8192, 1024], P('req', 'kv'), may hold values from -0.0625 to 0.0625
- value_projection_weight: bfloat16 [8192, 1024], P('req', 'kv'), may hold values from -0.0625 to 0.0625
- b_query: bfloat16 [8192], P('kv'), may hold values from -3 to 3
- key_bias: bfloat16 [1024], P('kv'), may hold values from -4.5 to 4.5
- value_bias: bfloat16 [1024], P('kv'), may hold values from -4.5 to 4.5
- w_out: bfloat16 [8192, 8192], P('req', 'kv'), may hold values from -0.0625 to 0.0625
- mlp_gain: bfloat16 [8192], P('kv'), may hold values from 0.099609375 to 1.8984375
- w_gate: bfloat16 [8192, 29568], P('kv', 'req'), may hold values from -0.0625 to 0.0625
- w_up: bfloat16 [8192, 29568], P('kv', 'req'), may hold values from -0.0625 to 0.0625
- w_down: bfloat16 [29568, 8192], P('req', 'kv'), may hold values from -0.03125 to 0.03125
Outputs:
- residual: float32 [128, 8192], P('req', 'kv')
Inputs may be any that keep to these rules, and one draw needn't show every extreme that they name: `request_serving_order`: A permutation of the requests. `cache_len`: in each layer the caches of the requests of one serving index of req sum to at most 8192 rows, and to exactly 8192 for one index; some request of that index has exactly 4096. `rotated_key_cache`: rows of an index beyond its requests' caches hold no cached tokens.
All inputs are finite; a program needn't handle non-finite values.
Results may differ from a plain program's by a relative error of at most 0.015.
Values may be sent and summed in bfloat16 or wider, within the bound.
No kernel may reach another device: no remote copies, remote signals or barrier semaphores. Data moves between devices by JAX's collectives and lax.ppermute only.
A program may use at most 256 MiB of HBM per device.

v0:
```python
import math
import jax
import jax.numpy as jnp
from jax import lax
from jax.sharding import PartitionSpec as P

MODEL_WIDTH = 8192
HEAD_SIZE = 128
LAYER_COUNT = 2
EPS = 1e-06
LOG_BASE = math.log(1000000.0)


def broadcast(block, axis, owner):
    block = jnp.where(lax.axis_index(axis) == owner, block, jnp.zeros_like(block))
    return lax.psum(block, axis)


def apply_rotation(values, token_positions):
    half_width = values.shape[-1] // 2
    frequency = jnp.exp(
        -LOG_BASE * jnp.arange(half_width, dtype=jnp.float32) * 2.0 / values.shape[-1]
    )
    angles = token_positions[:, None] * frequency[None, :]
    reshape_to = (angles.shape[0],) + (1,) * (values.ndim - 2) + (half_width,)
    cosine = jnp.cos(angles).reshape(reshape_to)
    sine_part = jnp.sin(angles).reshape(reshape_to)
    front_half = values[..., :half_width]
    back_half = values[..., half_width:]
    return jnp.concatenate(
        [front_half * cosine - back_half * sine_part, back_half * cosine + front_half * sine_part],
        axis=-1,
    )


def normalize(residual, gains):
    square_sum = jnp.sum(residual * residual, axis=1)
    all_squares = lax.psum(square_sum, "kv")
    inv_norm = lax.rsqrt(all_squares / MODEL_WIDTH + EPS)
    return (residual * inv_norm[:, None] * gains.astype(jnp.float32)[None, :]).astype(jnp.bfloat16)


def attend(query_rows, fresh_key, fresh_value, cached_keys, cached_values, lengths):
    score_scale = 1.0 / math.sqrt(query_rows.shape[-1])
    finish = jnp.cumsum(lengths)
    starts = finish - lengths
    capacity = cached_keys.shape[0]
    block_size = min(512, capacity)
    block_count = capacity // block_size
    self_score = (
        jnp.einsum("igrd,igd->igr", query_rows, fresh_key, preferred_element_type=jnp.float32)
        * score_scale
    )
    start_out = fresh_value.astype(jnp.float32)[:, :, None, :] * jnp.ones(
        query_rows.shape, jnp.float32
    )

    def one_block(block_index, carried):
        running_max, running_sum, accumulated = carried
        first_row = block_index * block_size
        key_block = lax.dynamic_slice_in_dim(cached_keys, first_row, block_size, 0)
        value_block = lax.dynamic_slice_in_dim(cached_values, first_row, block_size, 0)
        scores = (
            jnp.einsum("igrd,tgd->igrt", query_rows, key_block, preferred_element_type=jnp.float32)
            * score_scale
        )
        key_rows = first_row + jnp.arange(block_size, dtype=jnp.int32)
        inside = (key_rows[None, :] >= starts[:, None]) & (key_rows[None, :] < finish[:, None])
        inside = inside[:, None, None, :]
        block_max = jnp.max(jnp.where(inside, scores, -jnp.inf), axis=-1)
        new_max = jnp.maximum(running_max, block_max)
        exps = jnp.where(inside, jnp.exp(scores - new_max[..., None]), 0.0)
        rescale = jnp.exp(running_max - new_max)
        new_sum = running_sum * rescale + jnp.sum(exps, axis=-1)
        contribution = jnp.einsum(
            "igrt,tgd->igrd",
            exps.astype(jnp.bfloat16),
            value_block,
            preferred_element_type=jnp.float32,
        )
        return (new_max, new_sum, accumulated * rescale[..., None] + contribution)

    running_max, running_sum, accumulated = lax.fori_loop(
        0, block_count, one_block, (self_score, jnp.ones_like(self_score), start_out)
    )
    return (accumulated / running_sum[..., None]).astype(jnp.bfloat16)


def body(
    hidden,
    cache_len,
    request_serving_order,
    rotated_key_cache,
    stored_value_cache,
    attn_gain,
    w_query,
    key_projection_weight,
    value_projection_weight,
    b_query,
    key_bias,
    value_bias,
    w_out,
    mlp_gain,
    w_gate,
    w_up,
    w_down,
):
    req_size = lax.axis_size("req")
    kv_size = lax.axis_size("kv")
    group_ratio = req_size // kv_size
    req_index = lax.axis_index("req")
    own_rows = hidden.shape[0]
    head_dim = HEAD_SIZE
    query_width = w_query.shape[1]
    key_width = key_projection_weight.shape[1]
    kv_heads = key_width // head_dim
    capacity = rotated_key_cache.shape[1]
    w_joint = jnp.concatenate([w_query, key_projection_weight, value_projection_weight], axis=1)
    b_joint = jnp.concatenate([b_query, key_bias, value_bias]).astype(jnp.float32)
    inverse = jnp.argsort(request_serving_order)
    my_slots = lax.dynamic_slice_in_dim(request_serving_order, req_index * own_rows, own_rows)
    residual = hidden.astype(jnp.float32)
    for current_layer_index in range(LAYER_COUNT):
        normed = normalize(residual, attn_gain)
        gathered = lax.all_gather(normed, "req", axis=0, tiled=True)
        slab_width = gathered.shape[1] // group_ratio
        portion = lax.dynamic_slice_in_dim(
            gathered, req_index % group_ratio * slab_width, slab_width, 1
        )
        columns = broadcast(portion, "kv", req_index // group_ratio)
        picked = jnp.take(columns, request_serving_order, axis=0)
        combined = (
            lax.psum_scatter(
                jnp.dot(picked, w_joint, preferred_element_type=jnp.float32),
                "req",
                scatter_dimension=0,
                tiled=True,
            )
            + b_joint[None, :]
        )
        lengths = jnp.take(cache_len[current_layer_index], my_slots)
        token_positions = lengths.astype(jnp.float32)
        query_rows = apply_rotation(
            combined[:, :query_width].reshape(own_rows, kv_heads, -1, head_dim), token_positions
        ).astype(jnp.bfloat16)
        fresh_key = apply_rotation(
            combined[:, query_width : query_width + key_width].reshape(
                own_rows, kv_heads, head_dim
            ),
            token_positions,
        ).astype(jnp.bfloat16)
        fresh_value = (
            combined[:, query_width + key_width :]
            .reshape(own_rows, kv_heads, head_dim)
            .astype(jnp.bfloat16)
        )
        cached_keys = rotated_key_cache[current_layer_index].reshape(capacity, kv_heads, head_dim)
        cached_values = stored_value_cache[current_layer_index].reshape(
            capacity, kv_heads, head_dim
        )
        attention_output = attend(
            query_rows, fresh_key, fresh_value, cached_keys, cached_values, lengths
        ).reshape(own_rows, query_width)
        heads_gathered = lax.all_gather(attention_output, "req", axis=0, tiled=True)
        head_width = heads_gathered.shape[1] // group_ratio
        head_portion = lax.dynamic_slice_in_dim(
            heads_gathered, req_index % group_ratio * head_width, head_width, 1
        )
        head_rows = broadcast(head_portion, "kv", req_index // group_ratio)
        project_picked = jnp.take(head_rows, inverse, axis=0)
        residual = residual + lax.psum_scatter(
            jnp.dot(project_picked, w_out, preferred_element_type=jnp.float32),
            "req",
            scatter_dimension=0,
            tiled=True,
        )
        normed_mlp = normalize(residual, mlp_gain)
        tokens = lax.all_gather(normed_mlp, "req", axis=0, tiled=True)
        hidden_cols = w_gate.shape[1]
        gate_up = lax.psum_scatter(
            jnp.concatenate(
                [
                    jnp.dot(tokens, w_gate, preferred_element_type=jnp.float32),
                    jnp.dot(tokens, w_up, preferred_element_type=jnp.float32),
                ],
                axis=1,
            ),
            "kv",
            scatter_dimension=0,
            tiled=True,
        )
        local_hidden = (jax.nn.silu(gate_up[:, :hidden_cols]) * gate_up[:, hidden_cols:]).astype(
            jnp.bfloat16
        )
        hidden_all = lax.all_gather(local_hidden, "kv", axis=0, tiled=True)
        residual = residual + lax.psum_scatter(
            jnp.dot(hidden_all, w_down, preferred_element_type=jnp.float32),
            "req",
            scatter_dimension=0,
            tiled=True,
        )
    return residual


def solution(mesh):
    return jax.shard_map(
        body,
        mesh=mesh,
        in_specs=(
            P("req", "kv"),
            P(),
            P(),
            P(None, "req", "kv"),
            P(None, "req", "kv"),
            P("kv"),
            P("req", "kv"),
            P("req", "kv"),
            P("req", "kv"),
            P("kv"),
            P("kv"),
            P("kv"),
            P("req", "kv"),
            P("kv"),
            P("kv", "req"),
            P("kv", "req"),
            P("req", "kv"),
        ),
        out_specs=P("req", "kv"),
        check_vma=False,
    )
```

profile of v0, /device:TPU:0, one launch (start us, length us, event | category | flops | bytes accessed | tf_op | source)
XLA Modules:
  0.0 851.7 jit_solution(730094470468017407)
XLA Ops:
  8.2 13.5 %psum.56 = f32[16]{0:T(128)S(1)} all-reduce(f32[16]{0:T(128)S(1)} %fusion.46), channel_id=1, replica_groups=mesh['req'=8,'kv'=4] {'kv'}, use_global_device_ids=true, to_apply=%region_1.2 | all-reduce | flops 16 | bytes 128 | tf_op jit(solution)/shard_map/psum | solution.py:38
  22.6 9.9 %all_gather.24 = bf16[128,2048]{1,0:T(8,128)(2,1)S(1)} all-gather(bf16[16,2048]{1,0:T(8,128)(2,1)S(1)} %fusion.48), channel_id=1, replica_groups=mesh['req'=8,'kv'=4] {'req'}, dimensions={0}, use_global_device_ids=true | all-gather | bytes 589824 | tf_op jit(solution)/shard_map/all_gather | solution.py:125
  54.9 11.1 %all-reduce.5.cloned.1.call-done = bf16[128,1024]{1,0:T(8,128)(2,1)} async-done(((bf16[128,1024]{1,0:T(8,128)(2,1)}), bf16[128,1024]{1,0:T(8,128)(2,1)}) %all-reduce.5.cloned.1.call-update) | async-done | bytes 262160 | tf_op jit(solution)/shard_map/psum | solution.py:16
  87.9 21.9 %reduce-scatter.13.cloned.1.call-done = f32[16,2560]{1,0:T(8,128)} async-done(((f32[128,2560]{1,0:T(8,128)}), f32[16,2560]{1,0:T(8,128)}) %reduce-scatter.13.cloned.1.call-update) | async-done | bytes 163856 | tf_op jit(solution)/shard_map/reduce_scatter | solution.py:133
  111.6 46.3 %while.36 = (s32[]{:T(128)}, f32[16,2,8]{0,2,1:T(8,128)S(1)}, f32[16,2,8]{0,2,1:T(8,128)S(1)}, f32[16,2,8,128]{3,0,2,1:T(8,128)S(1)}, s32[16]{0:T(128)S(1)}, /*i...) while((s32[]{:T(128)}, f32[16,2,8]{0,2,1:T(8,128)S(1)}, ...), condition=%wide.region_8.11_spmd.clone, body=%wide.region_5.10_spmd.clone.sunk | while | flops 68379904 | bytes 2478401 | solution.py:83
  158.1 9.8 %all_gather.25 = bf16[128,2048]{1,0:T(8,128)(2,1)S(1)} all-gather(bf16[16,2048]{1,0:T(8,128)(2,1)S(1)} %bitcast.130), channel_id=1, replica_groups=mesh['req'=8,'kv'=4] {'req'}, dimensions={0}, use_global_device_ids=true | all-gather | bytes 589824 | tf_op jit(solution)/shard_map/all_gather | solution.py:164
  168.7 35.4 %all-reduce.7.cloned.1.call-done = bf16[128,1024]{1,0:T(8,128)(2,1)} async-done(((bf16[128,1024]{1,0:T(8,128)(2,1)}), bf16[128,1024]{1,0:T(8,128)(2,1)}) %all-reduce.7.cloned.1.call-update) | async-done | bytes 262160 | tf_op jit(solution)/shard_map/psum | solution.py:16
  210.2 35.9 %reduce-scatter.15.cloned.1.call-done = f32[16,2048]{1,0:T(8,128)} async-done(((f32[128,2048]{1,0:T(8,128)}), f32[16,2048]{1,0:T(8,128)}) %reduce-scatter.15.cloned.1.call-update) | async-done | bytes 131088 | tf_op jit(solution)/shard_map/reduce_scatter | solution.py:171
  247.1 11.7 %psum.59 = f32[16]{0:T(128)S(1)} all-reduce(f32[16]{0:T(128)S(1)} %multiply_reduce_fusion.2), channel_id=1, replica_groups=mesh['req'=8,'kv'=4] {'kv'}, use_global_device_ids=true, to_apply=%region_13.16 | all-reduce | flops 16 | bytes 128 | tf_op jit(solution)/shard_map/psum | solution.py:38
  259.8 10.0 %all_gather.26 = bf16[128,2048]{1,0:T(8,128)(2,1)S(1)} all-gather(bf16[16,2048]{1,0:T(8,128)(2,1)S(1)} %multiply_convert_fusion.2), channel_id=1, replica_groups=mesh['req'=8,'kv'=4] {'req'}, dimensions={0}, use_global_device_ids=true | all-gather | bytes 589824 | tf_op jit(solution)/shard_map/all_gather | solution.py:178
  269.7 7.6 fusion.75
  277.4 7.6 fusion.76
  292.4 67.9 %reduce-scatter.25.cloned.1.call-done = f32[32,7392]{1,0:T(8,128)} async-done(((f32[128,7392]{1,0:T(8,128)}), f32[32,7392]{1,0:T(8,128)}) %reduce-scatter.25.cloned.1.call-update) | async-done | bytes 946192 | tf_op jit(solution)/shard_map/reduce_scatter | solution.py:180
  361.7 20.5 %all_gather.27 = bf16[128,3696]{1,0:T(8,128)(2,1)S(1)} all-gather(bf16[32,3696]{1,0:T(8,128)(2,1)S(1)} %fusion.33), channel_id=1, replica_groups=mesh['req'=8,'kv'=4] {'kv'}, dimensions={0}, use_global_device_ids=true | all-gather | bytes 1182720 | tf_op jit(solution)/shard_map/all_gather | solution.py:195
  382.2 8.7 %fusion.77 = f32[128,2048]{1,0:T(8,128)} fusion(bf16[128,3696]{1,0:T(8,128)(2,1)S(1)} %all_gather.27, bf16[3696,2048]{1,0:T(8,128)(2,1)} %param.41), kind=kOutput, calls=%fused_computation.167 | convolution fusion | flops 1937768448 | bytes 17133568 | tf_op jit(solution)/shard_map/dot_general | solution.py:197
  391.0 36.1 %reduce-scatter.17.cloned.1.call-done = f32[16,2048]{1,0:T(8,128)} async-done(((f32[128,2048]{1,0:T(8,128)}), f32[16,2048]{1,0:T(8,128)}) %reduce-scatter.17.cloned.1.call-update) | async-done | bytes 131088 | tf_op jit(solution)/shard_map/reduce_scatter | solution.py:196
  428.2 11.7 %psum.60 = f32[16]{0:T(128)S(1)} all-reduce(f32[16]{0:T(128)S(1)} %get-tuple-element.479), channel_id=1, replica_groups=mesh['req'=8,'kv'=4] {'kv'}, use_global_device_ids=true, to_apply=%region_17.20 | all-reduce | flops 16 | bytes 128 | tf_op jit(solution)/shard_map/psum | solution.py:38
  440.0 9.8 %all_gather.28 = bf16[128,2048]{1,0:T(8,128)(2,1)S(1)} all-gather(bf16[16,2048]{1,0:T(8,128)(2,1)S(1)} %multiply_convert_fusion.1), channel_id=1, replica_groups=mesh['req'=8,'kv'=4] {'req'}, dimensions={0}, use_global_device_ids=true | all-gather | bytes 589824 | tf_op jit(solution)/shard_map/all_gather | solution.py:125
  450.6 32.7 %all-reduce.9.cloned.1.call-done = bf16[128,1024]{1,0:T(8,128)(2,1)} async-done(((bf16[128,1024]{1,0:T(8,128)(2,1)}), bf16[128,1024]{1,0:T(8,128)(2,1)}) %all-reduce.9.cloned.1.call-update) | async-done | bytes 262160 | tf_op jit(solution)/shard_map/psum | solution.py:16
  503.0 24.0 %reduce-scatter.19.cloned.1.call-done = f32[16,2560]{1,0:T(8,128)} async-done(((f32[128,2560]{1,0:T(8,128)}), f32[16,2560]{1,0:T(8,128)}) %reduce-scatter.19.cloned.1.call-update) | async-done | bytes 163856 | tf_op jit(solution)/shard_map/reduce_scatter | solution.py:133
  528.7 46.3 %while.37 = (s32[]{:T(128)}, f32[16,2,8]{0,2,1:T(8,128)S(1)}, f32[16,2,8]{0,2,1:T(8,128)S(1)}, f32[16,2,8,128]{3,0,2,1:T(8,128)S(1)}, s32[16]{0:T(128)S(1)}, /*i...) while((s32[]{:T(128)}, f32[16,2,8]{0,2,1:T(8,128)S(1)}, ...), condition=%wide.region_24.27_spmd.clone, body=%wide.region_21.26_spmd.clone.sunk | while | flops 68379904 | bytes 2478401 | solution.py:83
  575.3 9.8 %all_gather.29 = bf16[128,2048]{1,0:T(8,128)(2,1)S(1)} all-gather(bf16[16,2048]{1,0:T(8,128)(2,1)S(1)} %bitcast.131), channel_id=1, replica_groups=mesh['req'=8,'kv'=4] {'req'}, dimensions={0}, use_global_device_ids=true | all-gather | bytes 589824 | tf_op jit(solution)/shard_map/all_gather | solution.py:164
  585.9 35.4 %all-reduce.11.cloned.1.call-done = bf16[128,1024]{1,0:T(8,128)(2,1)} async-done(((bf16[128,1024]{1,0:T(8,128)(2,1)}), bf16[128,1024]{1,0:T(8,128)(2,1)}) %all-reduce.11.cloned.1.call-update) | async-done | bytes 262160 | tf_op jit(solution)/shard_map/psum | solution.py:16
  627.4 35.9 %reduce-scatter.21.cloned.1.call-done = f32[16,2048]{1,0:T(8,128)} async-done(((f32[128,2048]{1,0:T(8,128)}), f32[16,2048]{1,0:T(8,128)}) %reduce-scatter.21.cloned.1.call-update) | async-done | bytes 131088 | tf_op jit(solution)/shard_map/reduce_scatter | solution.py:171
  664.3 11.7 %psum.63 = f32[16]{0:T(128)S(1)} all-reduce(f32[16]{0:T(128)S(1)} %get-tuple-element.477), channel_id=1, replica_groups=mesh['req'=8,'kv'=4] {'kv'}, use_global_device_ids=true, to_apply=%region_28.31 | all-reduce | flops 16 | bytes 128 | tf_op jit(solution)/shard_map/psum | solution.py:38
  676.1 9.8 %all_gather.30 = bf16[128,2048]{1,0:T(8,128)(2,1)S(1)} all-gather(bf16[16,2048]{1,0:T(8,128)(2,1)S(1)} %multiply_convert_fusion), channel_id=1, replica_groups=mesh['req'=8,'kv'=4] {'req'}, dimensions={0}, use_global_device_ids=true | all-gather | bytes 589824 | tf_op jit(solution)/shard_map/all_gather | solution.py:178
  685.9 7.6 fusion.78
  693.6 7.6 fusion.79
  708.7 67.9 %reduce-scatter.27.cloned.1.call-done = f32[32,7392]{1,0:T(8,128)} async-done(((f32[128,7392]{1,0:T(8,128)}), f32[32,7392]{1,0:T(8,128)}) %reduce-scatter.27.cloned.1.call-update) | async-done | bytes 946192 | tf_op jit(solution)/shard_map/reduce_scatter | solution.py:180
  777.9 20.5 %all_gather.31 = bf16[128,3696]{1,0:T(8,128)(2,1)S(1)} all-gather(bf16[32,3696]{1,0:T(8,128)(2,1)S(1)} %fusion.32), channel_id=1, replica_groups=mesh['req'=8,'kv'=4] {'kv'}, dimensions={0}, use_global_device_ids=true | all-gather | bytes 1182720 | tf_op jit(solution)/shard_map/all_gather | solution.py:195
  798.4 8.7 %fusion.80 = f32[128,2048]{1,0:T(8,128)} fusion(bf16[128,3696]{1,0:T(8,128)(2,1)S(1)} %all_gather.31, bf16[3696,2048]{1,0:T(8,128)(2,1)} %param.41), kind=kOutput, calls=%fused_computation.170 | convolution fusion | flops 1937768448 | bytes 17133568 | tf_op jit(solution)/shard_map/dot_general | solution.py:197
  807.1 36.1 %reduce-scatter.23.cloned.1.call-done = f32[16,2048]{1,0:T(8,128)} async-done(((f32[128,2048]{1,0:T(8,128)}), f32[16,2048]{1,0:T(8,128)}) %reduce-scatter.23.cloned.1.call-update) | async-done | bytes 131088 | tf_op jit(solution)/shard_map/reduce_scatter | solution.py:196
  (404 shorter events, 198.8 us)
Async XLA Ops:
  6.5 59.5 %all-reduce.5.cloned.1.call-start = ((), (), s32[]{:S(2)}) async-start(), calls=%async_computation.8 | async-start | bytes 524288 | tf_op jit(solution)/shard_map/psum | solution.py:16
  33.3 76.5 %reduce-scatter.13.cloned.1.call-start = ((), (), s32[]{:S(2)}) async-start(), calls=%async_computation.9 | async-start | bytes 1474560 | tf_op jit(solution)/shard_map/reduce_scatter | solution.py:133
  34.0 4.9 copy-start.6
  34.0 4.9 copy-start.7
  40.2 5.9 copy-start.2
  40.2 6.8 copy-start.3
  72.5 131.6 %all-reduce.7.cloned.1.call-start = ((), (), s32[]{:S(2)}) async-start(), calls=%async_computation.10 | async-start | bytes 524288 | tf_op jit(solution)/shard_map/psum | solution.py:16
  78.4 9.2 %copy-start.4 = (bf16[2048]{0:T(1024)(128)(2,1)S(1)}, bf16[2048]{0:T(1024)(128)(2,1)}, u32[]{:S(2)}) copy-start(bf16[2048]{0:T(1024)(128)(2,1)} %param.34) | copy-start | bytes 12292
  78.4 9.2 %copy-start.8 = (bf16[256]{0:T(256)(128)(2,1)S(1)}, bf16[256]{0:T(256)(128)(2,1)}, u32[]{:S(2)}) copy-start(bf16[256]{0:T(256)(128)(2,1)} %param.36) | copy-start | bytes 1540
  78.4 9.2 %copy-start.9 = (bf16[256]{0:T(256)(128)(2,1)S(1)}, bf16[256]{0:T(256)(128)(2,1)}, u32[]{:S(2)}) copy-start(bf16[256]{0:T(256)(128)(2,1)} %param.35) | copy-start | bytes 1540
  168.6 77.4 %reduce-scatter.15.cloned.1.call-start = ((), (), s32[]{:S(2)}) async-start(), calls=%async_computation.11 | async-start | bytes 1179648 | tf_op jit(solution)/shard_map/reduce_scatter | solution.py:171
  168.7 41.4 %copy-start.5 = (bf16[2048]{0:T(1024)(128)(2,1)S(1)}, bf16[2048]{0:T(1024)(128)(2,1)}, u32[]{:S(2)}) copy-start(bf16[2048]{0:T(1024)(128)(2,1)} %param.38) | copy-start | bytes 12292
  168.7 77.3 %copy-start = (bf16[16,2048]{1,0:T(8,128)(2,1)S(1)}, bf16[16,2048]{1,0:T(8,128)(2,1)}, u32[]{:S(2)}) copy-start(bf16[16,2048]{1,0:T(8,128)(2,1)} %param.25) | copy-start | bytes 196612
  210.1 150.2 %reduce-scatter.25.cloned.1.call-start = ((), (), s32[]{:S(2)}) async-start(), calls=%async_computation.18 | async-start | bytes 4751360 | tf_op jit(solution)/shard_map/reduce_scatter | solution.py:180
  292.4 134.7 %reduce-scatter.17.cloned.1.call-start = ((), (), s32[]{:S(2)}) async-start(), calls=%async_computation.12 | async-start | bytes 1179648 | tf_op jit(solution)/shard_map/reduce_scatter | solution.py:196
  382.2 44.9 %copy-start.1 = (f32[16,2048]{1,0:T(8,128)S(1)}, f32[16,2048]{1,0:T(8,128)}, u32[]{:S(2)}) copy-start(f32[16,2048]{1,0:T(8,128)} %reduce-scatter.15.cloned.1.call-done) | copy-start | bytes 393220
  390.9 92.3 %all-reduce.9.cloned.1.call-start = ((), (), s32[]{:S(2)}) async-start(), calls=%async_computation.13 | async-start | bytes 524288 | tf_op jit(solution)/shard_map/psum | solution.py:16
  450.5 76.4 %reduce-scatter.19.cloned.1.call-start = ((), (), s32[]{:S(2)}) async-start(), calls=%async_computation.14 | async-start | bytes 1474560 | tf_op jit(solution)/shard_map/reduce_scatter | solution.py:133
  489.7 131.6 %all-reduce.11.cloned.1.call-start = ((), (), s32[]{:S(2)}) async-start(), calls=%async_computation.15 | async-start | bytes 524288 | tf_op jit(solution)/shard_map/psum | solution.py:16
  585.8 77.5 %reduce-scatter.21.cloned.1.call-start = ((), (), s32[]{:S(2)}) async-start(), calls=%async_computation.16 | async-start | bytes 1179648 | tf_op jit(solution)/shard_map/reduce_scatter | solution.py:171
  627.3 149.2 %reduce-scatter.27.cloned.1.call-start = ((), (), s32[]{:S(2)}) async-start(), calls=%async_computation.19 | async-start | bytes 4751360 | tf_op jit(solution)/shard_map/reduce_scatter | solution.py:180
  708.6 134.7 %reduce-scatter.23.cloned.1.call-start = ((), (), s32[]{:S(2)}) async-start(), calls=%async_computation.17 | async-start | bytes 1179648 | tf_op jit(solution)/shard_map/reduce_scatter | solution.py:196
Sparse Core Ops, SparseCore 0:
  33.4 32.5 all-reduce.4
  72.6 37.0 reduce-scatter.12
  168.7 35.3 all-reduce.6
  210.2 35.7 reduce-scatter.14
  292.5 67.7 reduce-scatter.24
  391.0 36.0 reduce-scatter.16
  450.6 32.5 all-reduce.8
  489.9 37.0 reduce-scatter.18
  585.9 35.3 all-reduce.10
  627.4 35.7 reduce-scatter.20
  708.7 67.7 reduce-scatter.26
  807.3 35.9 reduce-scatter.22
where the time goes:
time: 855 us; the launch traced here: 852 us
  waiting for transfers between devices  440 us (51%)
  blocking collectives  149 us (17%)
  matrix products  145 us (17%)
  local copies, waits for them, and re-layouts  65.2 us (8%)
  other arithmetic  35.7 us (4%)
  between operations  14 us (2%)
    reduce_scatter x2, waiting for transfers between devices, body(): lax.psum_scatter(jnp.concatenate([jnp.dot(tokens, w_gate, preferred_eleme...  136 us
    psum x4, waiting for transfers between devices, broadcast(): return lax.psum(block, axis)  115 us
    reduce_scatter x2, waiting for transfers between devices, body(): lax.psum_scatter(jnp.dot(hidden_all, w_down, preferred_element_type=jnp.f...  72.3 us
    reduce_scatter x2, waiting for transfers between devices, body(): lax.psum_scatter(jnp.dot(project_picked, w_out, preferred_element_type=jn...  71.8 us
    psum x4, blocking collectives, normalize(): all_squares = lax.psum(square_sum, 'kv')  48.6 us
    reduce_scatter x2, waiting for transfers between devices, body(): lax.psum_scatter(jnp.dot(picked, w_joint, preferred_element_type=jnp.floa...  45.9 us
    unnamed x34, local copies, waits for them, and re-layouts  42.4 us
    all_gather x2, blocking collectives, body(): hidden_all = lax.all_gather(local_hidden, 'kv', axis=0, tiled=True)  40.9 us
  transfers between devices with their start and end apart: 12, of which 12 were waited for; matrix products, arithmetic and copies ran while one was open for 6% of the time, Pallas kernels for 0%

commit v1 on v0

--- a/solution.py
+++ b/solution.py
@@ -13,7 +13,7 @@
 
 def broadcast(block, axis, owner):
     block = jnp.where(lax.axis_index(axis) == owner, block, jnp.zeros_like(block))
-    return lax.psum(block, axis)
+    return jnp.sum(lax.all_gather(block, axis), axis=0)
 
 
 def apply_rotation(values, token_positions):

time: 855 us -> 826 us (0.966)
  waiting for transfers between devices: 440 us -> 409 us
    psum x4 -> x0, waiting for transfers between devices: 115 us -> none  [broadcast(): return lax.psum(block, axis)]
    all_gather x0 -> x4, waiting for transfers between devices: none -> 81.7 us  [broadcast(): return jnp.sum(lax.all_gather(block, axis), axis=0)]
where the time goes in v1:
time: 826 us; the launch traced here: 822 us
  waiting for transfers between devices  409 us (50%)
  blocking collectives  148 us (18%)
  matrix products  145 us (18%)
  local copies, waits for them, and re-layouts  60.5 us (7%)
  other arithmetic  42.1 us (5%)
  between operations  14.1 us (2%)
    reduce_scatter x2, waiting for transfers between devices, body(): lax.psum_scatter(jnp.concatenate([jnp.dot(tokens, w_gate, preferred_eleme...  136 us
    all_gather x4, waiting for transfers between devices, broadcast(): return jnp.sum(lax.all_gather(block, axis), axis=0)  81.7 us
    reduce_scatter x2, waiting for transfers between devices, body(): lax.psum_scatter(jnp.dot(hidden_all, w_down, preferred_element_type=jnp.f...  72.2 us
    reduce_scatter x2, waiting for transfers between devices, body(): lax.psum_scatter(jnp.dot(project_picked, w_out, preferred_element_type=jn...  71.2 us
    psum x4, blocking collectives, normalize(): all_squares = lax.psum(square_sum, 'kv')  48.6 us
    reduce_scatter x2, waiting for transfers between devices, body(): lax.psum_scatter(jnp.dot(picked, w_joint, preferred_element_type=jnp.floa...  48.1 us
    unnamed x34, local copies, waits for them, and re-layouts  42.3 us
    all_gather x2, blocking collectives, body(): hidden_all = lax.all_gather(local_hidden, 'kv', axis=0, tiled=True)  40.9 us
  transfers between devices with their start and end apart: 12, of which 12 were waited for; matrix products, arithmetic and copies ran while one was open for 6% of the time, Pallas kernels for 0%

profile of v1, /device:TPU:0, one launch (start us, length us, event | category | flops | bytes accessed | tf_op | source)
XLA Modules:
  0.0 822.3 jit_solution(17421391369186156949)
XLA Ops:
  8.2 13.5 %psum.28 = f32[16]{0:T(128)S(1)} all-reduce(f32[16]{0:T(128)S(1)} %fusion.46), channel_id=1, replica_groups=mesh['req'=8,'kv'=4] {'kv'}, use_global_device_ids=true, to_apply=%region_1.2 | all-reduce | flops 16 | bytes 128 | tf_op jit(solution)/shard_map/psum | solution.py:38
  22.6 9.9 %all_gather.48 = bf16[128,2048]{1,0:T(8,128)(2,1)S(1)} all-gather(bf16[16,2048]{1,0:T(8,128)(2,1)S(1)} %fusion.48), channel_id=1, replica_groups=mesh['req'=8,'kv'=4] {'req'}, dimensions={0}, use_global_device_ids=true | all-gather | bytes 589824 | tf_op jit(solution)/shard_map/all_gather | solution.py:125
  71.4 6.5 copy.109
  78.2 24.2 %reduce-scatter.13.cloned.1.call-done = f32[16,2560]{1,0:T(8,128)} async-done(((f32[128,2560]{1,0:T(8,128)}), f32[16,2560]{1,0:T(8,128)}) %reduce-scatter.13.cloned.1.call-update) | async-done | bytes 163856 | tf_op jit(solution)/shard_map/reduce_scatter | solution.py:133
  104.2 46.3 %while.36 = (s32[]{:T(128)}, f32[16,2,8]{0,2,1:T(8,128)S(1)}, f32[16,2,8]{0,2,1:T(8,128)S(1)}, f32[16,2,8,128]{3,0,2,1:T(8,128)S(1)}, s32[16]{0:T(128)S(1)}, /*i...) while((s32[]{:T(128)}, f32[16,2,8]{0,2,1:T(8,128)S(1)}, ...), condition=%wide.region_8.11_spmd.clone, body=%wide.region_5.10_spmd.clone.sunk | while | flops 68379904 | bytes 2478401 | solution.py:83
  150.7 9.8 %all_gather.51 = bf16[128,2048]{1,0:T(8,128)(2,1)S(1)} all-gather(bf16[16,2048]{1,0:T(8,128)(2,1)S(1)} %bitcast.138), channel_id=1, replica_groups=mesh['req'=8,'kv'=4] {'req'}, dimensions={0}, use_global_device_ids=true | all-gather | bytes 589824 | tf_op jit(solution)/shard_map/all_gather | solution.py:164
  161.4 28.0 %all-gather.11.cloned.1.call-done = bf16[512,1024]{1,0:T(8,128)(2,1)} async-done(((bf16[128,1024]{1,0:T(8,128)(2,1)}), bf16[512,1024]{1,0:T(8,128)(2,1)}) %all-gather.11.cloned.1.call-update) | async-done | bytes 1048592 | tf_op jit(solution)/shard_map/all_gather | solution.py:16
  195.7 35.6 %reduce-scatter.15.cloned.1.call-done = f32[16,2048]{1,0:T(8,128)} async-done(((f32[128,2048]{1,0:T(8,128)}), f32[16,2048]{1,0:T(8,128)}) %reduce-scatter.15.cloned.1.call-update) | async-done | bytes 131088 | tf_op jit(solution)/shard_map/reduce_scatter | solution.py:171
  232.4 11.7 %psum.29 = f32[16]{0:T(128)S(1)} all-reduce(f32[16]{0:T(128)S(1)} %multiply_reduce_fusion.2), channel_id=1, replica_groups=mesh['req'=8,'kv'=4] {'kv'}, use_global_device_ids=true, to_apply=%region_13.16 | all-reduce | flops 16 | bytes 128 | tf_op jit(solution)/shard_map/psum | solution.py:38
  245.1 10.0 %all_gather.54 = bf16[128,2048]{1,0:T(8,128)(2,1)S(1)} all-gather(bf16[16,2048]{1,0:T(8,128)(2,1)S(1)} %multiply_convert_fusion.2), channel_id=1, replica_groups=mesh['req'=8,'kv'=4] {'req'}, dimensions={0}, use_global_device_ids=true | all-gather | bytes 589824 | tf_op jit(solution)/shard_map/all_gather | solution.py:178
  255.1 7.6 fusion.75
  262.7 7.6 fusion.76
  277.8 67.9 %reduce-scatter.25.cloned.1.call-done = f32[32,7392]{1,0:T(8,128)} async-done(((f32[128,7392]{1,0:T(8,128)}), f32[32,7392]{1,0:T(8,128)}) %reduce-scatter.25.cloned.1.call-update) | async-done | bytes 946192 | tf_op jit(solution)/shard_map/reduce_scatter | solution.py:180
  347.0 20.5 %all_gather.55 = bf16[128,3696]{1,0:T(8,128)(2,1)S(1)} all-gather(bf16[32,3696]{1,0:T(8,128)(2,1)S(1)} %fusion.33), channel_id=1, replica_groups=mesh['req'=8,'kv'=4] {'kv'}, dimensions={0}, use_global_device_ids=true | all-gather | bytes 1182720 | tf_op jit(solution)/shard_map/all_gather | solution.py:195
  367.5 8.7 %fusion.77 = f32[128,2048]{1,0:T(8,128)} fusion(bf16[128,3696]{1,0:T(8,128)(2,1)S(1)} %all_gather.55, bf16[3696,2048]{1,0:T(8,128)(2,1)} %param.41), kind=kOutput, calls=%fused_computation.167 | convolution fusion | flops 1937768448 | bytes 17133568 | tf_op jit(solution)/shard_map/dot_general | solution.py:197
  376.3 36.1 %reduce-scatter.17.cloned.1.call-done = f32[16,2048]{1,0:T(8,128)} async-done(((f32[128,2048]{1,0:T(8,128)}), f32[16,2048]{1,0:T(8,128)}) %reduce-scatter.17.cloned.1.call-update) | async-done | bytes 131088 | tf_op jit(solution)/shard_map/reduce_scatter | solution.py:196
  413.4 11.7 %psum.30 = f32[16]{0:T(128)S(1)} all-reduce(f32[16]{0:T(128)S(1)} %get-tuple-element.479), channel_id=1, replica_groups=mesh['req'=8,'kv'=4] {'kv'}, use_global_device_ids=true, to_apply=%region_17.20 | all-reduce | flops 16 | bytes 128 | tf_op jit(solution)/shard_map/psum | solution.py:38
  425.3 9.8 %all_gather.56 = bf16[128,2048]{1,0:T(8,128)(2,1)S(1)} all-gather(bf16[16,2048]{1,0:T(8,128)(2,1)S(1)} %multiply_convert_fusion.1), channel_id=1, replica_groups=mesh['req'=8,'kv'=4] {'req'}, dimensions={0}, use_global_device_ids=true | all-gather | bytes 589824 | tf_op jit(solution)/shard_map/all_gather | solution.py:125
  435.9 25.3 %all-gather.13.cloned.1.call-done = bf16[512,1024]{1,0:T(8,128)(2,1)} async-done(((bf16[128,1024]{1,0:T(8,128)(2,1)}), bf16[512,1024]{1,0:T(8,128)(2,1)}) %all-gather.13.cloned.1.call-update) | async-done | bytes 1048592 | tf_op jit(solution)/shard_map/all_gather | solution.py:16
  481.1 23.9 %reduce-scatter.19.cloned.1.call-done = f32[16,2560]{1,0:T(8,128)} async-done(((f32[128,2560]{1,0:T(8,128)}), f32[16,2560]{1,0:T(8,128)}) %reduce-scatter.19.cloned.1.call-update) | async-done | bytes 163856 | tf_op jit(solution)/shard_map/reduce_scatter | solution.py:133
  506.7 46.3 %while.37 = (s32[]{:T(128)}, f32[16,2,8]{0,2,1:T(8,128)S(1)}, f32[16,2,8]{0,2,1:T(8,128)S(1)}, f32[16,2,8,128]{3,0,2,1:T(8,128)S(1)}, s32[16]{0:T(128)S(1)}, /*i...) while((s32[]{:T(128)}, f32[16,2,8]{0,2,1:T(8,128)S(1)}, ...), condition=%wide.region_24.27_spmd.clone, body=%wide.region_21.26_spmd.clone.sunk | while | flops 68379904 | bytes 2478401 | solution.py:83
  553.2 9.8 %all_gather.59 = bf16[128,2048]{1,0:T(8,128)(2,1)S(1)} all-gather(bf16[16,2048]{1,0:T(8,128)(2,1)S(1)} %bitcast.139), channel_id=1, replica_groups=mesh['req'=8,'kv'=4] {'req'}, dimensions={0}, use_global_device_ids=true | all-gather | bytes 589824 | tf_op jit(solution)/shard_map/all_gather | solution.py:164
  563.9 28.1 %all-gather.15.cloned.1.call-done = bf16[512,1024]{1,0:T(8,128)(2,1)} async-done(((bf16[128,1024]{1,0:T(8,128)(2,1)}), bf16[512,1024]{1,0:T(8,128)(2,1)}) %all-gather.15.cloned.1.call-update) | async-done | bytes 1048592 | tf_op jit(solution)/shard_map/all_gather | solution.py:16
  598.2 35.6 %reduce-scatter.21.cloned.1.call-done = f32[16,2048]{1,0:T(8,128)} async-done(((f32[128,2048]{1,0:T(8,128)}), f32[16,2048]{1,0:T(8,128)}) %reduce-scatter.21.cloned.1.call-update) | async-done | bytes 131088 | tf_op jit(solution)/shard_map/reduce_scatter | solution.py:171
  634.9 11.7 %psum.31 = f32[16]{0:T(128)S(1)} all-reduce(f32[16]{0:T(128)S(1)} %get-tuple-element.477), channel_id=1, replica_groups=mesh['req'=8,'kv'=4] {'kv'}, use_global_device_ids=true, to_apply=%region_28.31 | all-reduce | flops 16 | bytes 128 | tf_op jit(solution)/shard_map/psum | solution.py:38
  646.7 9.8 %all_gather.62 = bf16[128,2048]{1,0:T(8,128)(2,1)S(1)} all-gather(bf16[16,2048]{1,0:T(8,128)(2,1)S(1)} %multiply_convert_fusion), channel_id=1, replica_groups=mesh['req'=8,'kv'=4] {'req'}, dimensions={0}, use_global_device_ids=true | all-gather | bytes 589824 | tf_op jit(solution)/shard_map/all_gather | solution.py:178
  656.5 7.6 fusion.78
  664.1 7.6 fusion.79
  679.2 67.9 %reduce-scatter.27.cloned.1.call-done = f32[32,7392]{1,0:T(8,128)} async-done(((f32[128,7392]{1,0:T(8,128)}), f32[32,7392]{1,0:T(8,128)}) %reduce-scatter.27.cloned.1.call-update) | async-done | bytes 946192 | tf_op jit(solution)/shard_map/reduce_scatter | solution.py:180
  748.5 20.5 %all_gather.63 = bf16[128,3696]{1,0:T(8,128)(2,1)S(1)} all-gather(bf16[32,3696]{1,0:T(8,128)(2,1)S(1)} %fusion.32), channel_id=1, replica_groups=mesh['req'=8,'kv'=4] {'kv'}, dimensions={0}, use_global_device_ids=true | all-gather | bytes 1182720 | tf_op jit(solution)/shard_map/all_gather | solution.py:195
  769.0 8.7 %fusion.80 = f32[128,2048]{1,0:T(8,128)} fusion(bf16[128,3696]{1,0:T(8,128)(2,1)S(1)} %all_gather.63, bf16[3696,2048]{1,0:T(8,128)(2,1)} %param.41), kind=kOutput, calls=%fused_computation.170 | convolution fusion | flops 1937768448 | bytes 17133568 | tf_op jit(solution)/shard_map/dot_general | solution.py:197
  777.7 36.2 %reduce-scatter.23.cloned.1.call-done = f32[16,2048]{1,0:T(8,128)} async-done(((f32[128,2048]{1,0:T(8,128)}), f32[16,2048]{1,0:T(8,128)}) %reduce-scatter.23.cloned.1.call-update) | async-done | bytes 131088 | tf_op jit(solution)/shard_map/reduce_scatter | solution.py:196
  (407 shorter events, 194.4 us)
Async XLA Ops:
  6.5 52.1 %all-gather.9.cloned.1.call-start = ((), (), s32[]{:S(2)}) async-start(), calls=%async_computation.14 | async-start | bytes 1310720 | tf_op jit(solution)/shard_map/all_gather | solution.py:16
  33.2 69.2 %reduce-scatter.13.cloned.1.call-start = ((), (), s32[]{:S(2)}) async-start(), calls=%async_computation.8 | async-start | bytes 1474560 | tf_op jit(solution)/shard_map/reduce_scatter | solution.py:133
  37.3 6.0 copy-start.7
  37.3 7.3 copy-start.4
  51.6 4.9 copy-start.2
  51.6 5.8 copy-start.3
  65.4 124.0 %all-gather.11.cloned.1.call-start = ((), (), s32[]{:S(2)}) async-start(), calls=%async_computation.15 | async-start | bytes 1310720 | tf_op jit(solution)/shard_map/all_gather | solution.py:16
  71.3 6.6 copy-start.5
  71.3 6.6 copy-start.8
  71.4 6.6 copy-start.9
  161.3 70.1 %reduce-scatter.15.cloned.1.call-start = ((), (), s32[]{:S(2)}) async-start(), calls=%async_computation.9 | async-start | bytes 1179648 | tf_op jit(solution)/shard_map/reduce_scatter | solution.py:171
  190.8 4.9 copy-start.6
  190.8 40.5 %copy-start = (bf16[16,2048]{1,0:T(8,128)(2,1)S(1)}, bf16[16,2048]{1,0:T(8,128)(2,1)}, u32[]{:S(2)}) copy-start(bf16[16,2048]{1,0:T(8,128)(2,1)} %param.25) | copy-start | bytes 196612
  195.7 150.0 %reduce-scatter.25.cloned.1.call-start = ((), (), s32[]{:S(2)}) async-start(), calls=%async_computation.18 | async-start | bytes 4751360 | tf_op jit(solution)/shard_map/reduce_scatter | solution.py:180
  277.7 134.7 %reduce-scatter.17.cloned.1.call-start = ((), (), s32[]{:S(2)}) async-start(), calls=%async_computation.10 | async-start | bytes 1179648 | tf_op jit(solution)/shard_map/reduce_scatter | solution.py:196
  367.5 44.9 %copy-start.1 = (f32[16,2048]{1,0:T(8,128)S(1)}, f32[16,2048]{1,0:T(8,128)}, u32[]{:S(2)}) copy-start(f32[16,2048]{1,0:T(8,128)} %reduce-scatter.15.cloned.1.call-done) | copy-start | bytes 393220
  376.3 84.9 %all-gather.13.cloned.1.call-start = ((), (), s32[]{:S(2)}) async-start(), calls=%async_computation.16 | async-start | bytes 1310720 | tf_op jit(solution)/shard_map/all_gather | solution.py:16
  435.8 69.1 %reduce-scatter.19.cloned.1.call-start = ((), (), s32[]{:S(2)}) async-start(), calls=%async_computation.11 | async-start | bytes 1474560 | tf_op jit(solution)/shard_map/reduce_scatter | solution.py:133
  467.9 124.0 %all-gather.15.cloned.1.call-start = ((), (), s32[]{:S(2)}) async-start(), calls=%async_computation.17 | async-start | bytes 1310720 | tf_op jit(solution)/shard_map/all_gather | solution.py:16
  563.8 70.0 %reduce-scatter.21.cloned.1.call-start = ((), (), s32[]{:S(2)}) async-start(), calls=%async_computation.12 | async-start | bytes 1179648 | tf_op jit(solution)/shard_map/reduce_scatter | solution.py:171
  598.2 149.0 %reduce-scatter.27.cloned.1.call-start = ((), (), s32[]{:S(2)}) async-start(), calls=%async_computation.19 | async-start | bytes 4751360 | tf_op jit(solution)/shard_map/reduce_scatter | solution.py:180
  679.2 134.7 %reduce-scatter.23.cloned.1.call-start = ((), (), s32[]{:S(2)}) async-start(), calls=%async_computation.13 | async-start | bytes 1179648 | tf_op jit(solution)/shard_map/reduce_scatter | solution.py:196
Sparse Core Ops, SparseCore 0:
  33.4 25.2 all-gather.8
  65.5 36.8 reduce-scatter.12
  161.4 27.9 all-gather.10
  195.8 35.5 reduce-scatter.14
  277.8 67.7 reduce-scatter.24
  376.4 35.9 reduce-scatter.16
  435.9 25.1 all-gather.12
  468.0 36.8 reduce-scatter.18
  563.9 27.9 all-gather.14
  598.3 35.4 reduce-scatter.20
  679.3 67.7 reduce-scatter.26
  777.8 35.9 reduce-scatter.22
